TPU v7x, 32 devices: a whole 2x2x4 slice. The times are simulated.
32 devices in a mesh: groups: 2 (over y), cam: 4 (over z), tm: 2 (over x), chan: 2 (over core).
Axes of the slice: x: 2, y: 2, z: 4, core: 2. Of those that a mesh axis runs over, the one named last changes fastest.
Arguments:
- video: bfloat16 [16, 8, 16, 8, 256], P(('groups', 'cam'), 'tm', None, None, 'chan'), parts along dimension 0, may hold values from -6 to 6
- conv_weight: bfloat16 [27, 256, 256], P(None, None, 'chan'), may hold values from -0.078125 to 0.078125
- proj_weight: bfloat16 [256, 16], P('chan'), may hold values from -0.375 to 0.375
- rig_sizes: int32 [8], P('groups'), parts along dimension 0, may hold values from 1 to 3, as said below
- camera_order: int32 [16], P('groups'), parts along dimension 0, may hold values from 0 to 7, as said below
- owner_slot: int32 [8], P('groups'), parts along dimension 0, may hold values from 0 to 3, as said below
- cotangent: bfloat16 [8, 8, 16, 128], P(('groups', 'cam'), 'tm'), parts along dimension 0, may hold values from -6 to 6
Outputs:
- robot_latent: float32 [8, 8, 16, 128], P(('groups', 'cam'), 'tm'), parts along dimension 0
- grad_conv: bfloat16 [54, 256, 256], P('groups', None, 'chan'), parts along dimension 0
- grad_proj: float32 [512, 16], P(('groups', 'chan')), parts along dimension 0
- grad_video: bfloat16 [16, 8, 16, 8, 256], P(('groups', 'cam'), 'tm', None, None, 'chan'), parts along dimension 0
There are 2 independent parts, one for each index of `groups`. A program takes and returns all parts, laid end to end along the dimension named above; an argument that names none is the same for every part. Nothing has to cross between parts.
Inputs may be any that keep to these rules, and one draw needn't show every extreme that they name: `rig_sizes`: the sizes sum to 8; the largest is exactly 3. `camera_order`: A permutation; the cameras whose places fall from rig_sizes[0] + ... + rig_sizes[r-1] to below rig_sizes[0] + ... + rig_sizes[r] belong to robot r. `owner_slot`: A permutation of the output rows.
All inputs are finite; a program needn't handle non-finite values.
Results may differ from a plain program's by a relative error of at most 0.0059.
Values may be sent and summed in bfloat16 or wider, within the bound.
No kernel may reach another device: no remote copies, remote signals or barrier semaphores. Data moves between devices by JAX's collectives and lax.ppermute only.
A program may use at most 128 MiB of HBM per device.

v0:
```python
import jax
import jax.numpy as jnp
from jax import lax
from jax.sharding import PartitionSpec as P

KT = 3
KS = 3


def shifted(shard, axis, by):
    size = lax.axis_size(axis)
    pairs = [(i, i + by) for i in range(size) if 0 <= i + by < size]
    return lax.ppermute(shard, axis, pairs)


def tap_offsets():
    return [
        (shift_t, shift_h, shift_w)
        for shift_t in range(KT)
        for shift_h in range(KS)
        for shift_w in range(KS)
    ]


def forward_taps(extended, weight, frames, height, width):
    channels = extended.shape[-1]
    summed = jnp.zeros((extended.shape[0] * frames * height * width, weight.shape[2]), jnp.float32)
    for tap_index, (shift_t, shift_h, shift_w) in enumerate(tap_offsets()):
        window = extended[
            :, shift_t : shift_t + frames, shift_h : shift_h + height, shift_w : shift_w + width, :
        ].reshape(-1, channels)
        summed = summed + jnp.dot(window, weight[tap_index], preferred_element_type=jnp.float32)
    return summed


def weight_taps(extended, grad_rows, frames, height, width):
    channels = extended.shape[-1]
    results = []
    for shift_t, shift_h, shift_w in tap_offsets():
        window = extended[
            :, shift_t : shift_t + frames, shift_h : shift_h + height, shift_w : shift_w + width, :
        ].reshape(-1, channels)
        results.append(
            lax.dot_general(
                window, grad_rows, (((0,), (0,)), ((), ())), preferred_element_type=jnp.float32
            )
        )
    return jnp.stack(results)


def input_taps(grad_rows, weight, batch, frames, height, width):
    channels = weight.shape[1]
    pad_half = KS // 2
    padded = jnp.zeros(
        (batch, frames + KT - 1, height + KS - 1, width + KS - 1, channels), jnp.float32
    )
    for tap_index, (shift_t, shift_h, shift_w) in enumerate(tap_offsets()):
        backed = lax.dot_general(
            grad_rows,
            weight[tap_index],
            (((1,), (1,)), ((), ())),
            preferred_element_type=jnp.float32,
        )
        padded = padded.at[
            :, shift_t : shift_t + frames, shift_h : shift_h + height, shift_w : shift_w + width, :
        ].add(backed.reshape(batch, frames, height, width, channels))
    return padded[:, :, pad_half : pad_half + height, pad_half : pad_half + width, :]


def joining_matrix(rig_sizes, camera_order, owner_slot):
    robots = rig_sizes.shape[0]
    ends = jnp.cumsum(rig_sizes)
    robot_of = jnp.sum((ends[None, :] <= camera_order[:, None]).astype(jnp.int32), axis=1)
    member = robot_of[:, None] == jnp.arange(robots, dtype=jnp.int32)[None, :]
    slot_of = jnp.sum(jnp.where(member, owner_slot[None, :], 0), axis=1)
    count_of = jnp.sum(jnp.where(member, rig_sizes[None, :], 0), axis=1)
    share = 1.0 / count_of.astype(jnp.float32)
    placed = slot_of[None, :] == jnp.arange(robots, dtype=jnp.int32)[:, None]
    return jnp.where(placed, share[None, :], jnp.zeros_like(share)[None, :])


def body(video, conv_weight, proj_weight, rig_sizes, camera_order, owner_slot, cotangent):
    cam_dev, frames, height, width, half_chan = video.shape
    pad_half = KS // 2
    lat_width = proj_weight.shape[1]
    cache_half = shifted(video[:, frames - (KT - 1) :], "tm", 1)
    whole_now, whole_cache = (
        lax.all_gather(video, "chan", axis=4, tiled=True),
        lax.all_gather(cache_half, "chan", axis=4, tiled=True),
    )
    extended = jnp.concatenate([whole_cache, whole_now], axis=1)
    extended = jnp.pad(
        extended, ((0, 0), (0, 0), (pad_half, pad_half), (pad_half, pad_half), (0, 0))
    )
    pre = forward_taps(extended, conv_weight, frames, height, width)
    sigma = jax.nn.sigmoid(pre)
    act = (pre * sigma).astype(jnp.bfloat16)
    latent_part = jnp.dot(act, proj_weight, preferred_element_type=jnp.float32)
    latent = lax.psum(latent_part, "chan").astype(jnp.bfloat16)
    mixing = joining_matrix(rig_sizes, camera_order, owner_slot)
    cam_index = lax.axis_index("cam")
    my_row = lax.dynamic_slice_in_dim(mixing, cam_index, 1, 0)
    latent_maps = latent.reshape(cam_dev, frames, height, width * lat_width)
    block_in = lax.all_gather(latent_maps, "cam", axis=0, tiled=True)
    count_in = block_in.shape[0]
    flat_in = block_in.reshape(count_in, -1).astype(jnp.float32)
    added = jnp.dot(
        my_row, flat_in, precision=lax.Precision.HIGHEST, preferred_element_type=jnp.float32
    )
    robot_latent = added.reshape(
        jnp.zeros((1, frames, height, width * lat_width), jnp.float32).shape
    )
    my_cols = lax.dynamic_slice_in_dim(mixing, cam_index * cam_dev, cam_dev, 1)
    block_in = lax.all_gather(cotangent, "cam", axis=0, tiled=True)
    count_in = block_in.shape[0]
    flat_in = block_in.reshape(count_in, -1).astype(jnp.float32)
    spread = lax.dot_general(
        my_cols,
        flat_in,
        (((0,), (0,)), ((), ())),
        precision=lax.Precision.HIGHEST,
        preferred_element_type=jnp.float32,
    )
    dlatent = spread.astype(jnp.bfloat16).reshape(-1, lat_width)
    grad_proj_local = lax.dot_general(
        act, dlatent, (((0,), (0,)), ((), ())), preferred_element_type=jnp.float32
    )
    dact = lax.dot_general(
        dlatent, proj_weight, (((1,), (1,)), ((), ())), preferred_element_type=jnp.float32
    )
    dpre = (dact * sigma * (1.0 + pre * (1.0 - sigma))).astype(jnp.bfloat16)
    full_back = input_taps(dpre, conv_weight, cam_dev, frames, height, width)
    cache_part = full_back[:, : KT - 1]
    incoming = shifted(cache_part, "tm", -1)
    own_part = full_back[:, KT - 1 :]
    own_part = own_part.at[:, frames - (KT - 1) :].add(incoming)
    grad_conv_local = weight_taps(extended, dpre, frames, height, width)
    grad_conv, grad_proj = lax.psum((grad_conv_local, grad_proj_local), ("cam", "tm"))
    grad_video = lax.psum_scatter(
        own_part.astype(jnp.bfloat16), "chan", scatter_dimension=4, tiled=True
    )
    return (robot_latent, grad_conv.astype(jnp.bfloat16), grad_proj, grad_video)


def solution(mesh):
    return jax.shard_map(
        body,
        mesh=mesh,
        in_specs=(
            P(("groups", "cam"), "tm", None, None, "chan"),
            P(None, None, "chan"),
            P("chan", None),
            P("groups"),
            P("groups"),
            P("groups"),
            P(("groups", "cam"), "tm", None, None),
        ),
        out_specs=(
            P(("groups", "cam"), "tm", None, None),
            P("groups", None, "chan"),
            P(("groups", "chan"), None),
            P(("groups", "cam"), "tm", None, None, "chan"),
        ),
        check_vma=False,
    )
```

profile of v0, /device:TPU:0, one launch (start us, length us, event | category | flops | bytes accessed | tf_op | source)
XLA Modules:
  0.0 450.1 jit_solution(12302339504369722204)
XLA Ops:
  8.2 4.8 %collective-permute-start = (bf16[2,2,16,8,128]{4,3,2,1,0:T(8,128)(2,1)S(1)}, bf16[2,2,16,8,128]{4,3,2,1,0:T(8,128)(2,1)S(1)}, u32[]{:S(2)}, u32[]{:S(2)}) collective-permute-start(bf16[2,2,16,8,128]{4,3,2,1,0:T(8,128)(2,1)S(1)} %slice.1486), channel_id=1, source_target_pairs={{0,2},{1,3},{4,6},{5,7},{8,10},{9,11},{12,14},{13,15},{16,18},{17,... | collective-permute-start | bytes 393224 | tf_op jit(solution)/shard_map/ppermute | solution.py:13
  15.4 13.6 %all_gather.15 = bf16[4,4,16,128]{3,2,1,0:T(8,128)(2,1)S(1)} all-gather(bf16[1,4,16,128]{3,2,1,0:T(8,128)(2,1)} %param.69), channel_id=1, replica_groups=mesh['groups'=2,'cam'=4,'tm'=2,'chan'=2] {'cam'}, dimensions={0}, use_global_device_ids=true | all-gather | bytes 81920 | tf_op jit(solution)/shard_map/all_gather | solution.py:114
  60.3 6.7 %scatter-add.95 = f32[2,6,18,10,256]{4,3,2,1,0:T(8,128)} dynamic-update-slice(f32[2,6,18,10,256]{4,3,2,1,0:T(8,128)} %scatter-add.94, f32[2,4,16,8,256]{4,3,2,1,0:T(8,128)S(1)} %convolution_add_fusion.25, s32[]{:T(128)} %constant.917.clone.1, s32[]{:T(128)} %constant.917.clone.1, s32[]{:T(128)} %constant.917.clone.1, s32[]{:T(128)} %constant.926.clone.1, s32[]{:T(128)} %constant.917.clone.1) | dynamic-update-slice | bytes 2097156 | tf_op jit(solution)/shard_map/scatter-add | solution.py:66
  68.9 6.7 %scatter-add.96 = f32[2,6,18,10,256]{4,3,2,1,0:T(8,128)} dynamic-update-slice(f32[2,6,18,10,256]{4,3,2,1,0:T(8,128)} %scatter-add.95, f32[2,4,16,8,256]{4,3,2,1,0:T(8,128)S(1)} %convolution_add_fusion.24, s32[]{:T(128)} %constant.917.clone.1, s32[]{:T(128)} %constant.917.clone.1, s32[]{:T(128)} %constant.917.clone.1, s32[]{:T(128)} %constant.924.clone.1, s32[]{:T(128)} %constant.917.clone.1) | dynamic-update-slice | bytes 2097156 | tf_op jit(solution)/shard_map/scatter-add | solution.py:66
  80.0 6.7 %scatter-add.100 = f32[2,6,18,10,256]{4,3,2,1,0:T(8,128)} dynamic-update-slice(f32[2,6,18,10,256]{4,3,2,1,0:T(8,128)} %fusion.7, f32[2,4,16,8,256]{4,3,2,1,0:T(8,128)S(1)} %convolution_add_fusion.22, s32[]{:T(128)} %constant.917.clone.1, s32[]{:T(128)} %constant.917.clone.1, s32[]{:T(128)} %constant.926.clone.1, s32[]{:T(128)} %constant.926.clone.1, s32[]{:T(128)} %constant.917.clone.1) | dynamic-update-slice | bytes 2097156 | tf_op jit(solution)/shard_map/scatter-add | solution.py:66
  86.7 3.8 convolution_add_fusion.21
  90.5 8.6 %scatter-add.101 = f32[2,6,18,10,256]{4,3,2,1,0:T(8,128)} dynamic-update-slice(f32[2,6,18,10,256]{4,3,2,1,0:T(8,128)} %scatter-add.100, f32[2,4,16,8,256]{4,3,2,1,0:T(8,128)S(1)} %convolution_add_fusion.21, s32[]{:T(128)} %constant.917.clone.1, s32[]{:T(128)} %bitcast.103, s32[]{:T(128)} %bitcast.104, s32[]{:T(128)} %bitcast.105, s32[]{:T(128)} %constant.917.clone.1) | dynamic-update-slice | bytes 2097156 | tf_op jit(solution)/shard_map/scatter-add | solution.py:66
  99.1 2.6 fusion.6
  103.6 6.7 %scatter-add.105 = f32[2,6,18,10,256]{4,3,2,1,0:T(8,128)} dynamic-update-slice(f32[2,6,18,10,256]{4,3,2,1,0:T(8,128)} %fusion.6, f32[2,4,16,8,256]{4,3,2,1,0:T(8,128)S(1)} %convolution_add_fusion.19, s32[]{:T(128)} %constant.917.clone.1, s32[]{:T(128)} %constant.917.clone.1, s32[]{:T(128)} %constant.924.clone.1, s32[]{:T(128)} %constant.926.clone.1, s32[]{:T(128)} %constant.917.clone.1) | dynamic-update-slice | bytes 2097156 | tf_op jit(solution)/shard_map/scatter-add | solution.py:66
  112.2 6.7 %scatter-add.106 = f32[2,6,18,10,256]{4,3,2,1,0:T(8,128)} dynamic-update-slice(f32[2,6,18,10,256]{4,3,2,1,0:T(8,128)} %scatter-add.105, f32[2,4,16,8,256]{4,3,2,1,0:T(8,128)S(1)} %convolution_add_fusion.18, s32[]{:T(128)} %constant.917.clone.1, s32[]{:T(128)} %constant.917.clone.1, s32[]{:T(128)} %constant.924.clone.1, s32[]{:T(128)} %constant.924.clone.1, s32[]{:T(128)} %constant.917.clone.1) | dynamic-update-slice | bytes 2097156 | tf_op jit(solution)/shard_map/scatter-add | solution.py:66
  118.9 2.7 fusion.5
  123.4 6.8 %scatter-add.110 = f32[2,6,18,10,256]{4,3,2,1,0:T(8,128)} dynamic-update-slice(f32[2,6,18,10,256]{4,3,2,1,0:T(8,128)} %fusion.5, f32[2,4,16,8,256]{4,3,2,1,0:T(8,128)S(1)} %convolution_add_fusion.16, s32[]{:T(128)} %constant.917.clone.1, s32[]{:T(128)} %constant.926.clone.1, s32[]{:T(128)} %constant.917.clone.1, s32[]{:T(128)} %constant.926.clone.1, s32[]{:T(128)} %constant.917.clone.1) | dynamic-update-slice | bytes 2097156 | tf_op jit(solution)/shard_map/scatter-add | solution.py:66
  132.1 6.8 %scatter-add.111 = f32[2,6,18,10,256]{4,3,2,1,0:T(8,128)} dynamic-update-slice(f32[2,6,18,10,256]{4,3,2,1,0:T(8,128)} %scatter-add.110, f32[2,4,16,8,256]{4,3,2,1,0:T(8,128)S(1)} %convolution_add_fusion.15, s32[]{:T(128)} %constant.917.clone.1, s32[]{:T(128)} %constant.926.clone.1, s32[]{:T(128)} %constant.917.clone.1, s32[]{:T(128)} %constant.924.clone.1, s32[]{:T(128)} %constant.917.clone.1) | dynamic-update-slice | bytes 2097156 | tf_op jit(solution)/shard_map/scatter-add | solution.py:66
  138.9 2.7 fusion.4
  143.4 6.7 %scatter-add.115 = f32[2,6,18,10,256]{4,3,2,1,0:T(8,128)} dynamic-update-slice(f32[2,6,18,10,256]{4,3,2,1,0:T(8,128)} %fusion.4, f32[2,4,16,8,256]{4,3,2,1,0:T(8,128)S(1)} %convolution_add_fusion.13, s32[]{:T(128)} %constant.917.clone.1, s32[]{:T(128)} %constant.926.clone.1, s32[]{:T(128)} %constant.926.clone.1, s32[]{:T(128)} %constant.926.clone.1, s32[]{:T(128)} %constant.917.clone.1) | dynamic-update-slice | bytes 2097156 | tf_op jit(solution)/shard_map/scatter-add | solution.py:66
  152.0 6.7 %scatter-add.116 = f32[2,6,18,10,256]{4,3,2,1,0:T(8,128)} dynamic-update-slice(f32[2,6,18,10,256]{4,3,2,1,0:T(8,128)} %scatter-add.115, f32[2,4,16,8,256]{4,3,2,1,0:T(8,128)S(1)} %convolution_add_fusion.12, s32[]{:T(128)} %constant.917.clone.1, s32[]{:T(128)} %constant.926.clone.1, s32[]{:T(128)} %constant.926.clone.1, s32[]{:T(128)} %constant.924.clone.1, s32[]{:T(128)} %constant.917.clone.1) | dynamic-update-slice | bytes 2097156 | tf_op jit(solution)/shard_map/scatter-add | solution.py:66
  158.8 2.7 fusion.3
  163.3 6.7 %scatter-add.120 = f32[2,6,18,10,256]{4,3,2,1,0:T(8,128)} dynamic-update-slice(f32[2,6,18,10,256]{4,3,2,1,0:T(8,128)} %fusion.3, f32[2,4,16,8,256]{4,3,2,1,0:T(8,128)S(1)} %convolution_add_fusion.10, s32[]{:T(128)} %constant.917.clone.1, s32[]{:T(128)} %constant.926.clone.1, s32[]{:T(128)} %constant.924.clone.1, s32[]{:T(128)} %constant.926.clone.1, s32[]{:T(128)} %constant.917.clone.1) | dynamic-update-slice | bytes 2097156 | tf_op jit(solution)/shard_map/scatter-add | solution.py:66
  172.0 6.7 %scatter-add.121 = f32[2,6,18,10,256]{4,3,2,1,0:T(8,128)} dynamic-update-slice(f32[2,6,18,10,256]{4,3,2,1,0:T(8,128)} %scatter-add.120, f32[2,4,16,8,256]{4,3,2,1,0:T(8,128)S(1)} %convolution_add_fusion.9, s32[]{:T(128)} %constant.917.clone.1, s32[]{:T(128)} %constant.926.clone.1, s32[]{:T(128)} %constant.924.clone.1, s32[]{:T(128)} %constant.924.clone.1, s32[]{:T(128)} %constant.917.clone.1) | dynamic-update-slice | bytes 2097156 | tf_op jit(solution)/shard_map/scatter-add | solution.py:66
  183.2 6.7 %scatter-add.125 = f32[2,6,18,10,256]{4,3,2,1,0:T(8,128)} dynamic-update-slice(f32[2,6,18,10,256]{4,3,2,1,0:T(8,128)} %fusion.2, f32[2,4,16,8,256]{4,3,2,1,0:T(8,128)S(1)} %convolution_add_fusion.7, s32[]{:T(128)} %constant.917.clone.1, s32[]{:T(128)} %constant.924.clone.1, s32[]{:T(128)} %constant.917.clone.1, s32[]{:T(128)} %constant.926.clone.1, s32[]{:T(128)} %constant.917.clone.1) | dynamic-update-slice | bytes 2097156 | tf_op jit(solution)/shard_map/scatter-add | solution.py:66
  191.8 6.7 %scatter-add.126 = f32[2,6,18,10,256]{4,3,2,1,0:T(8,128)} dynamic-update-slice(f32[2,6,18,10,256]{4,3,2,1,0:T(8,128)} %scatter-add.125, f32[2,4,16,8,256]{4,3,2,1,0:T(8,128)S(1)} %convolution_add_fusion.6, s32[]{:T(128)} %constant.917.clone.1, s32[]{:T(128)} %constant.924.clone.1, s32[]{:T(128)} %constant.917.clone.1, s32[]{:T(128)} %constant.924.clone.1, s32[]{:T(128)} %constant.917.clone.1) | dynamic-update-slice | bytes 2097156 | tf_op jit(solution)/shard_map/scatter-add | solution.py:66
  203.0 7.0 %scatter-add.130 = f32[2,6,18,10,256]{4,3,2,1,0:T(8,128)} dynamic-update-slice(f32[2,6,18,10,256]{4,3,2,1,0:T(8,128)} %fusion.1, f32[2,4,16,8,256]{4,3,2,1,0:T(8,128)S(1)} %convolution_add_fusion.4, s32[]{:T(128)} %constant.917.clone.1, s32[]{:T(128)} %constant.924.clone.1, s32[]{:T(128)} %constant.926.clone.1, s32[]{:T(128)} %constant.926.clone.1, s32[]{:T(128)} %constant.917.clone.1) | dynamic-update-slice | bytes 2097156 | tf_op jit(solution)/shard_map/scatter-add | solution.py:66
  211.9 6.7 %scatter-add.131 = f32[2,6,18,10,256]{4,3,2,1,0:T(8,128)} dynamic-update-slice(f32[2,6,18,10,256]{4,3,2,1,0:T(8,128)} %scatter-add.130, f32[2,4,16,8,256]{4,3,2,1,0:T(8,128)S(1)} %convolution_add_fusion.3, s32[]{:T(128)} %constant.917.clone.1, s32[]{:T(128)} %constant.924.clone.1, s32[]{:T(128)} %constant.926.clone.1, s32[]{:T(128)} %constant.924.clone.1, s32[]{:T(128)} %constant.917.clone.1) | dynamic-update-slice | bytes 2097156 | tf_op jit(solution)/shard_map/scatter-add | solution.py:66
  223.1 6.7 %scatter-add.135 = f32[2,6,18,10,256]{4,3,2,1,0:T(8,128)} dynamic-update-slice(f32[2,6,18,10,256]{4,3,2,1,0:T(8,128)} %fusion, f32[2,4,16,8,256]{4,3,2,1,0:T(8,128)S(1)} %convolution_add_fusion.1, s32[]{:T(128)} %constant.917.clone.1, s32[]{:T(128)} %constant.924.clone.1, s32[]{:T(128)} %constant.924.clone.1, s32[]{:T(128)} %constant.926.clone.1, s32[]{:T(128)} %constant.917.clone.1) | dynamic-update-slice | bytes 2097156 | tf_op jit(solution)/shard_map/scatter-add | solution.py:66
  231.7 6.7 %scatter-add.136 = f32[2,6,18,10,256]{4,3,2,1,0:T(8,128)} dynamic-update-slice(f32[2,6,18,10,256]{4,3,2,1,0:T(8,128)} %scatter-add.135, f32[2,4,16,8,256]{4,3,2,1,0:T(8,128)S(1)} %convolution_add_fusion, s32[]{:T(128)} %constant.917.clone.1, s32[]{:T(128)} %constant.924.clone.1, s32[]{:T(128)} %constant.924.clone.1, s32[]{:T(128)} %constant.924.clone.1, s32[]{:T(128)} %constant.917.clone.1) | dynamic-update-slice | bytes 2097156 | tf_op jit(solution)/shard_map/scatter-add | solution.py:66
  240.9 3.6 psum.21
  246.6 13.4 %all_gather.14 = bf16[8,4,16,128]{3,2,1,0:T(8,128)(2,1)S(1)} all-gather(bf16[2,4,16,128]{3,2,1,0:T(8,128)(2,1)S(1)} %reshape.1490), channel_id=1, replica_groups=mesh['groups'=2,'cam'=4,'tm'=2,'chan'=2] {'cam'}, dimensions={0}, use_global_device_ids=true | all-gather | bytes 163840 | tf_op jit(solution)/shard_map/all_gather | solution.py:104
  262.5 11.8 %copy.48 = bf16[2,4,16,8,256]{3,2,1,0,4:T(8,128)(2,1)} copy(bf16[2,4,16,8,256]{4,3,2,1,0:T(8,128)(2,1)S(1)} %fusion.37) | data formatting | bytes 1048576
  274.3 13.6 %reshape.1527 = bf16[256,1024]{1,0:T(8,128)(2,1)} reshape(bf16[256,2,4,16,8]{4,3,2,1,0:T(8,128)(2,1)} %bitcast.557) | data formatting | bytes 1048576
  288.0 142.3 %all-reduce.4 = (bf16[27,256,128]{2,1,0:T(8,128)(2,1)}, f32[128,16]{0,1:T(8,128)}) all-reduce(f32[27,256,128]{2,1,0:T(8,128)S(1)} %copy-done.4, f32[128,16]{0,1:T(8,128)S(1)} %fusion.156), channel_id=1, replica_groups=mesh['groups'=2,'cam'=4,'tm'=2,'chan'=2] {'cam','tm'}, use_global_device_ids=true, to_apply=%region_5.6 | all-reduce | flops 886784 | bytes 5324800 | tf_op jit(solution)/shard_map/psum | solution.py:138
  430.3 6.8 %reshape.1528 = bf16[128,2,4,16,8]{4,3,2,1,0:T(8,128)(2,1)} reshape(bf16[128,1024]{1,0:T(8,128)(2,1)} %reduce-scatter.4.cloned.1.call-done) | data formatting | bytes 524288
  437.2 6.1 %copy.49 = bf16[2,4,16,8,128]{4,3,2,1,0:T(8,128)(2,1)} copy(bf16[2,4,16,8,128]{3,2,1,0,4:T(8,128)(2,1)} %bitcast.558) | data formatting | bytes 524288
  (123 shorter events, 82.0 us)
Async XLA Ops:
  7.2 38.4 %copy-start = (bf16[128,16]{0,1:T(8,128)(2,1)S(1)}, bf16[128,16]{0,1:T(8,128)(2,1)}, u32[]{:S(2)}) copy-start(bf16[128,16]{0,1:T(8,128)(2,1)} %param.65) | copy-start | bytes 12292
  7.2 423.2 %reduce-scatter.4.cloned.1.call-start = ((), (), s32[]{:S(2)}) async-start(), calls=%async_computation.1 | async-start | bytes 786432
  8.2 24.4 %collective-permute-start = (bf16[2,2,16,8,128]{4,3,2,1,0:T(8,128)(2,1)S(1)}, bf16[2,2,16,8,128]{4,3,2,1,0:T(8,128)(2,1)S(1)}, u32[]{:S(2)}, u32[]{:S(2)}) collective-permute-start(bf16[2,2,16,8,128]{4,3,2,1,0:T(8,128)(2,1)S(1)} %slice.1486), channel_id=1, source_target_pairs={{0,2},{1,3},{4,6},{5,7},{8,10},{9,11},{12,14},{13,15},{16,18},{17,... | collective-permute-start | bytes 393224 | tf_op jit(solution)/shard_map/ppermute | solution.py:13
  35.0 2.3 copy-start.2
  45.6 2.2 copy-start.5
  55.7 1.8 copy-start.3
  229.8 31.2 %copy-start.6 = (bf16[1024,128]{1,0:T(8,128)(2,1)S(1)}, bf16[1024,128]{1,0:T(8,128)(2,1)}, u32[]{:S(2)}) copy-start(bf16[1024,128]{1,0:T(8,128)(2,1)} %copy-done.5) | copy-start | bytes 786436
  239.6 21.5 %collective-permute-start.1 = (f32[2,2,16,8,256]{4,3,2,1,0:T(8,128)S(1)}, f32[2,2,16,8,256]{4,3,2,1,0:T(8,128)S(1)}, u32[]{:S(2)}, u32[]{:S(2)}) collective-permute-start(f32[2,2,16,8,256]{4,3,2,1,0:T(8,128)S(1)} %slice.1599), channel_id=1, source_target_pairs={{2,0},{3,1},{6,4},{7,5},{10,8},{11,9},{14,12},{15,13},{18,16},{19,... | collective-permute-start | bytes 1572872 | tf_op jit(solution)/shard_map/ppermute | solution.py:13
  274.3 13.7 %copy-start.4 = (f32[27,256,128]{2,1,0:T(8,128)S(1)}, f32[27,256,128]{2,1,0:T(8,128)}, u32[]{:S(2)}) copy-start(f32[27,256,128]{2,1,0:T(8,128)} %copy-done.3) | copy-start | bytes 10616836
  288.0 155.3 %copy-start.1 = (bf16[128,16]{0,1:T(8,128)(2,1)S(1)}, bf16[128,16]{0,1:T(8,128)(2,1)}, u32[]{:S(2)}) copy-start(bf16[128,16]{0,1:T(8,128)(2,1)} %param.65) | copy-start | bytes 12292
Sparse Core Ops, SparseCore 0:
  288.1 10.2 reduce-scatter.3
where the time goes:
time: 454 us; the launch traced here: 450 us
  blocking collectives  177 us (39%)
  local copies, waits for them, and re-layouts  173 us (38%)
  matrix products  74.9 us (16%)
  between operations  14.6 us (3%)
  starting transfers between devices  6.18 us (1%)
    psum x1, blocking collectives, body(): lax.psum((grad_conv_local, grad_proj_local), ('cam', 'tm'))  142 us
    scatter-add x19, local copies, waits for them, and re-layouts, input_taps(): padded = padded.at[:, shift_t:shift_t + frames, shift_h:shift_h + height,...  125 us
    dot_general x27, matrix products, input_taps(): lax.dot_general(grad_rows, weight[tap_index], (((1,), (1,)), ((), ())), p...  55.4 us
    unnamed x20, local copies, waits for them, and re-layouts  40.4 us
    all_gather x1, blocking collectives, body(): block_in = lax.all_gather(cotangent, 'cam', axis=0, tiled=True)  13.6 us
    all_gather x1, blocking collectives, body(): block_in = lax.all_gather(latent_maps, 'cam', axis=0, tiled=True)  13.4 us
    dot_general x27, matrix products, weight_taps(): lax.dot_general(window, grad_rows, (((0,), (0,)), ((), ())), preferred_el...  9.49 us
  transfers between devices with their start and end apart: 3, of which 0 were waited for; matrix products, arithmetic and copies ran while one was open for 2% of the time, Pallas kernels for 0%

commit v1 on v0

--- a/solution.py
+++ b/solution.py
@@ -135,7 +135,7 @@
     own_part = full_back[:, KT - 1 :]
     own_part = own_part.at[:, frames - (KT - 1) :].add(incoming)
     grad_conv_local = weight_taps(extended, dpre, frames, height, width)
-    grad_conv, grad_proj = lax.psum((grad_conv_local, grad_proj_local), ("cam", "tm"))
+    grad_conv, grad_proj = lax.psum(lax.psum((grad_conv_local, grad_proj_local), "tm"), "cam")
     grad_video = lax.psum_scatter(
         own_part.astype(jnp.bfloat16), "chan", scatter_dimension=4, tiled=True
     )

time: 454 us -> 525 us (1.16)
  waiting for transfers between devices: 0.02 us -> 67.3 us
  matrix products: 74.9 us -> 85.4 us
  blocking collectives: 177 us -> 167 us
    psum x0 -> x1, waiting for transfers between devices: none -> 57.6 us  [body(): lax.psum((grad_conv_local, grad_proj_local), 'tm')]
    psum x1 -> x2, blocking collectives: 142 us -> 132 us  [the longest x1 127 us: body(): lax.psum(lax.psum((grad_conv_local, grad_proj_local), 'tm'), 'cam')]
    ppermute x2, waiting for transfers between devices: 0.01 us -> 9.63 us  [shifted(): return lax.ppermute(shard, axis, pairs)]
    unnamed x20 -> x38, local copies, waits for them, and re-layouts: 40.4 us -> 40.3 us
  transfers between devices with their start and end apart: 3 -> 4, of which waited for: 0 -> 2; matrix products, arithmetic and copies ran while one was open for 2% -> 5% of each run, Pallas kernels for 0% -> 0%
where the time goes in v1:
time: 525 us; the launch traced here: 521 us
  local copies, waits for them, and re-layouts  175 us (33%)
  blocking collectives  167 us (32%)
  matrix products  85.4 us (16%)
  waiting for transfers between devices  67.3 us (13%)
  between operations  16.1 us (3%)
  starting transfers between devices  6.48 us (1%)
    psum x1, blocking collectives, body(): lax.psum(lax.psum((grad_conv_local, grad_proj_local), 'tm'), 'cam')  127 us
    scatter-add x19, local copies, waits for them, and re-layouts, input_taps(): padded = padded.at[:, shift_t:shift_t + frames, shift_h:shift_h + height,...  127 us
    dot_general x27, matrix products, input_taps(): lax.dot_general(grad_rows, weight[tap_index], (((1,), (1,)), ((), ())), p...  60.3 us
    psum x1, waiting for transfers between devices, body(): lax.psum((grad_conv_local, grad_proj_local), 'tm')  57.6 us
    unnamed x38, local copies, waits for them, and re-layouts  40.3 us
    dot_general x27, matrix products, weight_taps(): lax.dot_general(window, grad_rows, (((0,), (0,)), ((), ())), preferred_el...  14.4 us
    all_gather x1, blocking collectives, body(): block_in = lax.all_gather(cotangent, 'cam', axis=0, tiled=True)  13.6 us
    all_gather x1, blocking collectives, body(): block_in = lax.all_gather(latent_maps, 'cam', axis=0, tiled=True)  13.4 us
  transfers between devices with their start and end apart: 4, of which 2 were waited for; matrix products, arithmetic and copies ran while one was open for 5% of the time, Pallas kernels for 0%

profile of v1, /device:TPU:0, one launch (start us, length us, event | category | flops | bytes accessed | tf_op | source)
XLA Modules:
  0.0 521.4 jit_solution(4568566891887017393)
XLA Ops:
  9.0 4.8 collective-permute-start
  16.2 13.6 %all_gather.15 = bf16[4,4,16,128]{3,2,1,0:T(8,128)(2,1)S(1)} all-gather(bf16[1,4,16,128]{3,2,1,0:T(8,128)(2,1)} %param.69), channel_id=1, replica_groups=mesh['groups'=2,'cam'=4,'tm'=2,'chan'=2] {'cam'}, dimensions={0}, use_global_device_ids=true | all-gather | bytes 81920 | tf_op jit(solution)/shard_map/all_gather | solution.py:114
  59.7 7.0 %scatter-add.95 = f32[2,6,18,10,256]{4,3,2,1,0:T(8,128)} dynamic-update-slice(f32[2,6,18,10,256]{4,3,2,1,0:T(8,128)} %scatter-add.94, f32[2,4,16,8,256]{4,3,2,1,0:T(8,128)} %convolution_add_fusion.25, s32[]{:T(128)} %constant.917.clone.1, s32[]{:T(128)} %constant.917.clone.1, s32[]{:T(128)} %constant.917.clone.1, s32[]{:T(128)} %constant.926.clone.1, s32[]{:T(128)} %constant.917.clone.1) | dynamic-update-slice | bytes 2097156 | tf_op jit(solution)/shard_map/scatter-add | solution.py:66
  69.5 7.0 %scatter-add.96 = f32[2,6,18,10,256]{4,3,2,1,0:T(8,128)} dynamic-update-slice(f32[2,6,18,10,256]{4,3,2,1,0:T(8,128)} %scatter-add.95, f32[2,4,16,8,256]{4,3,2,1,0:T(8,128)} %convolution_add_fusion.24, s32[]{:T(128)} %constant.917.clone.1, s32[]{:T(128)} %constant.917.clone.1, s32[]{:T(128)} %constant.917.clone.1, s32[]{:T(128)} %constant.924.clone.1, s32[]{:T(128)} %constant.917.clone.1) | dynamic-update-slice | bytes 2097156 | tf_op jit(solution)/shard_map/scatter-add | solution.py:66
  82.0 7.0 %scatter-add.100 = f32[2,6,18,10,256]{4,3,2,1,0:T(8,128)} dynamic-update-slice(f32[2,6,18,10,256]{4,3,2,1,0:T(8,128)} %fusion.7, f32[2,4,16,8,256]{4,3,2,1,0:T(8,128)} %convolution_add_fusion.22, s32[]{:T(128)} %constant.917.clone.1, s32[]{:T(128)} %constant.917.clone.1, s32[]{:T(128)} %constant.926.clone.1, s32[]{:T(128)} %constant.926.clone.1, s32[]{:T(128)} %constant.917.clone.1) | dynamic-update-slice | bytes 2097156 | tf_op jit(solution)/shard_map/scatter-add | solution.py:66
  89.1 4.8 convolution_add_fusion.21
  93.8 9.0 %scatter-add.101 = f32[2,6,18,10,256]{4,3,2,1,0:T(8,128)} dynamic-update-slice(f32[2,6,18,10,256]{4,3,2,1,0:T(8,128)} %scatter-add.100, f32[2,4,16,8,256]{4,3,2,1,0:T(8,128)} %convolution_add_fusion.21, s32[]{:T(128)} %constant.917.clone.1, s32[]{:T(128)} %bitcast.103, s32[]{:T(128)} %bitcast.104, s32[]{:T(128)} %bitcast.105, s32[]{:T(128)} %constant.917.clone.1) | dynamic-update-slice | bytes 2097156 | tf_op jit(solution)/shard_map/scatter-add | solution.py:66
  107.3 6.7 %scatter-add.105 = f32[2,6,18,10,256]{4,3,2,1,0:T(8,128)} dynamic-update-slice(f32[2,6,18,10,256]{4,3,2,1,0:T(8,128)} %fusion.6, f32[2,4,16,8,256]{4,3,2,1,0:T(8,128)S(1)} %convolution_add_fusion.19, s32[]{:T(128)} %constant.917.clone.1, s32[]{:T(128)} %constant.917.clone.1, s32[]{:T(128)} %constant.924.clone.1, s32[]{:T(128)} %constant.926.clone.1, s32[]{:T(128)} %constant.917.clone.1) | dynamic-update-slice | bytes 2097156 | tf_op jit(solution)/shard_map/scatter-add | solution.py:66
  115.9 6.7 %scatter-add.106 = f32[2,6,18,10,256]{4,3,2,1,0:T(8,128)} dynamic-update-slice(f32[2,6,18,10,256]{4,3,2,1,0:T(8,128)} %scatter-add.105, f32[2,4,16,8,256]{4,3,2,1,0:T(8,128)S(1)} %convolution_add_fusion.18, s32[]{:T(128)} %constant.917.clone.1, s32[]{:T(128)} %constant.917.clone.1, s32[]{:T(128)} %constant.924.clone.1, s32[]{:T(128)} %constant.924.clone.1, s32[]{:T(128)} %constant.917.clone.1) | dynamic-update-slice | bytes 2097156 | tf_op jit(solution)/shard_map/scatter-add | solution.py:66
  127.2 6.8 %scatter-add.110 = f32[2,6,18,10,256]{4,3,2,1,0:T(8,128)} dynamic-update-slice(f32[2,6,18,10,256]{4,3,2,1,0:T(8,128)} %fusion.5, f32[2,4,16,8,256]{4,3,2,1,0:T(8,128)S(1)} %convolution_add_fusion.16, s32[]{:T(128)} %constant.917.clone.1, s32[]{:T(128)} %constant.926.clone.1, s32[]{:T(128)} %constant.917.clone.1, s32[]{:T(128)} %constant.926.clone.1, s32[]{:T(128)} %constant.917.clone.1) | dynamic-update-slice | bytes 2097156 | tf_op jit(solution)/shard_map/scatter-add | solution.py:66
  135.9 6.8 %scatter-add.111 = f32[2,6,18,10,256]{4,3,2,1,0:T(8,128)} dynamic-update-slice(f32[2,6,18,10,256]{4,3,2,1,0:T(8,128)} %scatter-add.110, f32[2,4,16,8,256]{4,3,2,1,0:T(8,128)S(1)} %convolution_add_fusion.15, s32[]{:T(128)} %constant.917.clone.1, s32[]{:T(128)} %constant.926.clone.1, s32[]{:T(128)} %constant.917.clone.1, s32[]{:T(128)} %constant.924.clone.1, s32[]{:T(128)} %constant.917.clone.1) | dynamic-update-slice | bytes 2097156 | tf_op jit(solution)/shard_map/scatter-add | solution.py:66
  147.2 6.8 %scatter-add.115 = f32[2,6,18,10,256]{4,3,2,1,0:T(8,128)} dynamic-update-slice(f32[2,6,18,10,256]{4,3,2,1,0:T(8,128)} %fusion.4, f32[2,4,16,8,256]{4,3,2,1,0:T(8,128)S(1)} %convolution_add_fusion.13, s32[]{:T(128)} %constant.917.clone.1, s32[]{:T(128)} %constant.926.clone.1, s32[]{:T(128)} %constant.926.clone.1, s32[]{:T(128)} %constant.926.clone.1, s32[]{:T(128)} %constant.917.clone.1) | dynamic-update-slice | bytes 2097156 | tf_op jit(solution)/shard_map/scatter-add | solution.py:66
  155.9 6.8 %scatter-add.116 = f32[2,6,18,10,256]{4,3,2,1,0:T(8,128)} dynamic-update-slice(f32[2,6,18,10,256]{4,3,2,1,0:T(8,128)} %scatter-add.115, f32[2,4,16,8,256]{4,3,2,1,0:T(8,128)S(1)} %convolution_add_fusion.12, s32[]{:T(128)} %constant.917.clone.1, s32[]{:T(128)} %constant.926.clone.1, s32[]{:T(128)} %constant.926.clone.1, s32[]{:T(128)} %constant.924.clone.1, s32[]{:T(128)} %constant.917.clone.1) | dynamic-update-slice | bytes 2097156 | tf_op jit(solution)/shard_map/scatter-add | solution.py:66
  167.1 6.8 %scatter-add.120 = f32[2,6,18,10,256]{4,3,2,1,0:T(8,128)} dynamic-update-slice(f32[2,6,18,10,256]{4,3,2,1,0:T(8,128)} %fusion.3, f32[2,4,16,8,256]{4,3,2,1,0:T(8,128)S(1)} %convolution_add_fusion.10, s32[]{:T(128)} %constant.917.clone.1, s32[]{:T(128)} %constant.926.clone.1, s32[]{:T(128)} %constant.924.clone.1, s32[]{:T(128)} %constant.926.clone.1, s32[]{:T(128)} %constant.917.clone.1) | dynamic-update-slice | bytes 2097156 | tf_op jit(solution)/shard_map/scatter-add | solution.py:66
  175.8 6.8 %scatter-add.121 = f32[2,6,18,10,256]{4,3,2,1,0:T(8,128)} dynamic-update-slice(f32[2,6,18,10,256]{4,3,2,1,0:T(8,128)} %scatter-add.120, f32[2,4,16,8,256]{4,3,2,1,0:T(8,128)S(1)} %convolution_add_fusion.9, s32[]{:T(128)} %constant.917.clone.1, s32[]{:T(128)} %constant.926.clone.1, s32[]{:T(128)} %constant.924.clone.1, s32[]{:T(128)} %constant.924.clone.1, s32[]{:T(128)} %constant.917.clone.1) | dynamic-update-slice | bytes 2097156 | tf_op jit(solution)/shard_map/scatter-add | solution.py:66
  187.0 6.7 %scatter-add.125 = f32[2,6,18,10,256]{4,3,2,1,0:T(8,128)} dynamic-update-slice(f32[2,6,18,10,256]{4,3,2,1,0:T(8,128)} %fusion.2, f32[2,4,16,8,256]{4,3,2,1,0:T(8,128)S(1)} %convolution_add_fusion.7, s32[]{:T(128)} %constant.917.clone.1, s32[]{:T(128)} %constant.924.clone.1, s32[]{:T(128)} %constant.917.clone.1, s32[]{:T(128)} %constant.926.clone.1, s32[]{:T(128)} %constant.917.clone.1) | dynamic-update-slice | bytes 2097156 | tf_op jit(solution)/shard_map/scatter-add | solution.py:66
  195.6 6.7 %scatter-add.126 = f32[2,6,18,10,256]{4,3,2,1,0:T(8,128)} dynamic-update-slice(f32[2,6,18,10,256]{4,3,2,1,0:T(8,128)} %scatter-add.125, f32[2,4,16,8,256]{4,3,2,1,0:T(8,128)S(1)} %convolution_add_fusion.6, s32[]{:T(128)} %constant.917.clone.1, s32[]{:T(128)} %constant.924.clone.1, s32[]{:T(128)} %constant.917.clone.1, s32[]{:T(128)} %constant.924.clone.1, s32[]{:T(128)} %constant.917.clone.1) | dynamic-update-slice | bytes 2097156 | tf_op jit(solution)/shard_map/scatter-add | solution.py:66
  206.8 6.7 %scatter-add.130 = f32[2,6,18,10,256]{4,3,2,1,0:T(8,128)} dynamic-update-slice(f32[2,6,18,10,256]{4,3,2,1,0:T(8,128)} %fusion.1, f32[2,4,16,8,256]{4,3,2,1,0:T(8,128)S(1)} %convolution_add_fusion.4, s32[]{:T(128)} %constant.917.clone.1, s32[]{:T(128)} %constant.924.clone.1, s32[]{:T(128)} %constant.926.clone.1, s32[]{:T(128)} %constant.926.clone.1, s32[]{:T(128)} %constant.917.clone.1) | dynamic-update-slice | bytes 2097156 | tf_op jit(solution)/shard_map/scatter-add | solution.py:66
  215.3 6.7 %scatter-add.131 = f32[2,6,18,10,256]{4,3,2,1,0:T(8,128)} dynamic-update-slice(f32[2,6,18,10,256]{4,3,2,1,0:T(8,128)} %scatter-add.130, f32[2,4,16,8,256]{4,3,2,1,0:T(8,128)S(1)} %convolution_add_fusion.3, s32[]{:T(128)} %constant.917.clone.1, s32[]{:T(128)} %constant.924.clone.1, s32[]{:T(128)} %constant.926.clone.1, s32[]{:T(128)} %constant.924.clone.1, s32[]{:T(128)} %constant.917.clone.1) | dynamic-update-slice | bytes 2097156 | tf_op jit(solution)/shard_map/scatter-add | solution.py:66
  226.5 6.8 %scatter-add.135 = f32[2,6,18,10,256]{4,3,2,1,0:T(8,128)} dynamic-update-slice(f32[2,6,18,10,256]{4,3,2,1,0:T(8,128)} %fusion, f32[2,4,16,8,256]{4,3,2,1,0:T(8,128)S(1)} %convolution_add_fusion.1, s32[]{:T(128)} %constant.917.clone.1, s32[]{:T(128)} %constant.924.clone.1, s32[]{:T(128)} %constant.924.clone.1, s32[]{:T(128)} %constant.926.clone.1, s32[]{:T(128)} %constant.917.clone.1) | dynamic-update-slice | bytes 2097156 | tf_op jit(solution)/shard_map/scatter-add | solution.py:66
  233.3 2.9 convolution_add_fusion
  236.2 7.1 %scatter-add.136 = f32[2,6,18,10,256]{4,3,2,1,0:T(8,128)} dynamic-update-slice(f32[2,6,18,10,256]{4,3,2,1,0:T(8,128)} %scatter-add.135, f32[2,4,16,8,256]{4,3,2,1,0:T(8,128)} %convolution_add_fusion, s32[]{:T(128)} %constant.917.clone.1, s32[]{:T(128)} %constant.924.clone.1, s32[]{:T(128)} %constant.924.clone.1, s32[]{:T(128)} %constant.924.clone.1, s32[]{:T(128)} %constant.917.clone.1) | dynamic-update-slice | bytes 2097156 | tf_op jit(solution)/shard_map/scatter-add | solution.py:66
  250.8 9.6 %collective-permute-done.1 = f32[2,2,16,8,256]{4,3,2,1,0:T(8,128)S(1)} collective-permute-done((f32[2,2,16,8,256]{4,3,2,1,0:T(8,128)S(1)}, f32[2,2,16,8,256]{4,3,2,1,0:T(8,128)S(1)}, u32[]{:S(2)}, u32[]{:S(2)}) %collective-permute-start.1) | collective-permute-done | bytes 524320 | tf_op jit(solution)/shard_map/ppermute | solution.py:13
  261.7 11.8 %copy.48 = bf16[2,4,16,8,256]{3,2,1,0,4:T(8,128)(2,1)} copy(bf16[2,4,16,8,256]{4,3,2,1,0:T(8,128)(2,1)S(1)} %fusion.37) | data formatting | bytes 1048576
  273.5 13.6 %reshape.1527 = bf16[256,1024]{1,0:T(8,128)(2,1)} reshape(bf16[256,2,4,16,8]{4,3,2,1,0:T(8,128)(2,1)} %bitcast.557) | data formatting | bytes 1048576
  292.4 3.6 psum.35
  296.4 13.4 %all_gather.14 = bf16[8,4,16,128]{3,2,1,0:T(8,128)(2,1)S(1)} all-gather(bf16[2,4,16,128]{3,2,1,0:T(8,128)(2,1)S(1)} %reshape.1490), channel_id=1, replica_groups=mesh['groups'=2,'cam'=4,'tm'=2,'chan'=2] {'cam'}, dimensions={0}, use_global_device_ids=true | all-gather | bytes 163840 | tf_op jit(solution)/shard_map/all_gather | solution.py:104
  310.0 5.1 psum.38
  316.0 6.8 %reshape.1528 = bf16[128,2,4,16,8]{4,3,2,1,0:T(8,128)(2,1)} reshape(bf16[128,1024]{1,0:T(8,128)(2,1)} %reduce-scatter.4.cloned.1.call-done) | data formatting | bytes 524288
  322.9 6.1 %copy.49 = bf16[2,4,16,8,128]{4,3,2,1,0:T(8,128)(2,1)} copy(bf16[2,4,16,8,128]{3,2,1,0,4:T(8,128)(2,1)} %bitcast.558) | data formatting | bytes 524288
  329.0 57.6 %all-reduce.6.cloned.1.call-done = f32[27,256,128]{2,1,0:T(8,128)} async-done(((f32[27,256,128]{2,1,0:T(8,128)}), f32[27,256,128]{2,1,0:T(8,128)}) %all-reduce.6.cloned.1.call-update) | async-done | bytes 3538960 | tf_op jit(solution)/shard_map/psum | solution.py:138
  386.6 127.3 %all-reduce.7 = (bf16[27,256,128]{2,1,0:T(8,128)(2,1)}, f32[128,16]{0,1:T(8,128)}) all-reduce(f32[27,256,128]{2,1,0:T(8,128)} %all-reduce.6.cloned.1.call-done, f32[128,16]{0,1:T(8,128)S(1)} %psum.38), channel_id=1, replica_groups=mesh['groups'=2,'cam'=4,'tm'=2,'chan'=2] {'cam'}, use_global_device_ids=true, to_apply=%region_6.7 | all-reduce | flops 886784 | bytes 5324800 | tf_op jit(solution)/shard_map/psum | solution.py:138
  (145 shorter events, 99.4 us)
Async XLA Ops:
  8.0 39.2 %copy-start = (bf16[128,16]{0,1:T(8,128)(2,1)S(1)}, bf16[128,16]{0,1:T(8,128)(2,1)}, u32[]{:S(2)}) copy-start(bf16[128,16]{0,1:T(8,128)(2,1)} %param.65) | copy-start | bytes 12292
  8.0 308.0 %reduce-scatter.4.cloned.1.call-start = ((), (), s32[]{:S(2)}) async-start(), calls=%async_computation.2 | async-start | bytes 786432
  9.0 24.4 %collective-permute-start = (bf16[2,2,16,8,128]{4,3,2,1,0:T(8,128)(2,1)S(1)}, bf16[2,2,16,8,128]{4,3,2,1,0:T(8,128)(2,1)S(1)}, u32[]{:S(2)}, u32[]{:S(2)}) collective-permute-start(bf16[2,2,16,8,128]{4,3,2,1,0:T(8,128)(2,1)S(1)} %slice.1486), channel_id=1, source_target_pairs={{0,2},{1,3},{4,6},{5,7},{8,10},{9,11},{12,14},{13,15},{16,18},{17,... | collective-permute-start | bytes 393224 | tf_op jit(solution)/shard_map/ppermute | solution.py:13
  35.9 8.7 %copy-start.6 = (bf16[2,4,16,8,256]{4,3,2,1,0:T(8,128)(2,1)}, bf16[2,4,16,8,256]{4,3,2,1,0:T(8,128)(2,1)S(1)}, u32[]{:S(2)}) copy-start(bf16[2,4,16,8,256]{4,3,2,1,0:T(8,128)(2,1)S(1)} %get-tuple-element.364) | copy-start | bytes 1572868
  35.9 9.4 %copy-start.4 = (bf16[2,4,16,8,256]{4,3,2,1,0:T(8,128)(2,1)}, bf16[2,4,16,8,256]{4,3,2,1,0:T(8,128)(2,1)S(1)}, u32[]{:S(2)}) copy-start(bf16[2,4,16,8,256]{4,3,2,1,0:T(8,128)(2,1)S(1)} %get-tuple-element.365) | copy-start | bytes 1572868
  35.9 9.7 %copy-start.2 = (bf16[2,4,16,8,256]{4,3,2,1,0:T(8,128)(2,1)}, bf16[2,4,16,8,256]{4,3,2,1,0:T(8,128)(2,1)S(1)}, u32[]{:S(2)}) copy-start(bf16[2,4,16,8,256]{4,3,2,1,0:T(8,128)(2,1)S(1)} %get-tuple-element.366) | copy-start | bytes 1572868
  35.9 2.3 copy-start.1
  38.2 5.8 %copy-start.10 = (bf16[2,4,16,8,256]{4,3,2,1,0:T(8,128)(2,1)}, bf16[2,4,16,8,256]{4,3,2,1,0:T(8,128)(2,1)S(1)}, u32[]{:S(2)}) copy-start(bf16[2,4,16,8,256]{4,3,2,1,0:T(8,128)(2,1)S(1)} %get-tuple-element.361) | copy-start | bytes 1572868
  38.2 6.1 %copy-start.8 = (bf16[2,4,16,8,256]{4,3,2,1,0:T(8,128)(2,1)}, bf16[2,4,16,8,256]{4,3,2,1,0:T(8,128)(2,1)S(1)}, u32[]{:S(2)}) copy-start(bf16[2,4,16,8,256]{4,3,2,1,0:T(8,128)(2,1)S(1)} %get-tuple-element.362) | copy-start | bytes 1572868
  38.2 7.9 %copy-start.13 = (bf16[2,4,16,8,256]{4,3,2,1,0:T(8,128)(2,1)}, bf16[2,4,16,8,256]{4,3,2,1,0:T(8,128)(2,1)S(1)}, u32[]{:S(2)}) copy-start(bf16[2,4,16,8,256]{4,3,2,1,0:T(8,128)(2,1)S(1)} %get-tuple-element.344) | copy-start | bytes 1572868
  54.1 1.8 copy-start.12
  226.5 19.6 %copy-start.11 = (bf16[2,4,16,8,256]{4,3,2,1,0:T(8,128)(2,1)S(1)}, bf16[2,4,16,8,256]{4,3,2,1,0:T(8,128)(2,1)}, u32[]{:S(2)}) copy-start(bf16[2,4,16,8,256]{4,3,2,1,0:T(8,128)(2,1)} %copy-done.10) | copy-start | bytes 1572868
  233.2 15.5 %copy-start.9 = (bf16[2,4,16,8,256]{4,3,2,1,0:T(8,128)(2,1)S(1)}, bf16[2,4,16,8,256]{4,3,2,1,0:T(8,128)(2,1)}, u32[]{:S(2)}) copy-start(bf16[2,4,16,8,256]{4,3,2,1,0:T(8,128)(2,1)} %copy-done.8) | copy-start | bytes 1572868
  236.2 13.6 %copy-start.7 = (bf16[2,4,16,8,256]{4,3,2,1,0:T(8,128)(2,1)S(1)}, bf16[2,4,16,8,256]{4,3,2,1,0:T(8,128)(2,1)}, u32[]{:S(2)}) copy-start(bf16[2,4,16,8,256]{4,3,2,1,0:T(8,128)(2,1)} %copy-done.6) | copy-start | bytes 1572868
  244.5 15.9 %collective-permute-start.1 = (f32[2,2,16,8,256]{4,3,2,1,0:T(8,128)S(1)}, f32[2,2,16,8,256]{4,3,2,1,0:T(8,128)S(1)}, u32[]{:S(2)}, u32[]{:S(2)}) collective-permute-start(f32[2,2,16,8,256]{4,3,2,1,0:T(8,128)S(1)} %slice.1599), channel_id=1, source_target_pairs={{2,0},{3,1},{6,4},{7,5},{10,8},{11,9},{14,12},{15,13},{18,16},{19,... | collective-permute-start | bytes 1572872 | tf_op jit(solution)/shard_map/ppermute | solution.py:13
  273.5 14.7 %copy-start.5 = (bf16[2,4,16,8,256]{4,3,2,1,0:T(8,128)(2,1)S(1)}, bf16[2,4,16,8,256]{4,3,2,1,0:T(8,128)(2,1)}, u32[]{:S(2)}) copy-start(bf16[2,4,16,8,256]{4,3,2,1,0:T(8,128)(2,1)} %copy-done.4) | copy-start | bytes 1572868
  273.5 15.6 %copy-start.3 = (bf16[2,4,16,8,256]{4,3,2,1,0:T(8,128)(2,1)S(1)}, bf16[2,4,16,8,256]{4,3,2,1,0:T(8,128)(2,1)}, u32[]{:S(2)}) copy-start(bf16[2,4,16,8,256]{4,3,2,1,0:T(8,128)(2,1)} %copy-done.2) | copy-start | bytes 1572868
  287.1 4.0 copy-start.14
  287.1 99.5 %all-reduce.6.cloned.1.call-start = ((), (), s32[]{:S(2)}) async-start(), calls=%async_computation.1 | async-start | bytes 7077888 | tf_op jit(solution)/shard_map/psum | solution.py:138
  288.2 4.0 copy-start.15
Sparse Core Ops, SparseCore 0:
  287.3 8.0 reduce-scatter.3
Sparse Core Ops, SparseCore 1:
  292.3 94.3 all-reduce.5
